TPU v7x, 256 devices: a whole 4x4x8 slice. The times are simulated.
256 devices in a mesh: dp: 8 (over y, x_hi), expert: 8 (over z), tensor: 4 (over x_lo, core).
Axes of the slice: x: 4 (x_hi: 2, x_lo: 2; x = x_hi * 2 + x_lo), y: 4, z: 8, core: 2. Of those that a mesh axis runs over, the one named last changes fastest.
Arguments:
- tokens: bfloat16 [4096, 2048], P(('dp', 'expert', 'tensor')), may hold values from -6 to 6
- cotangent: bfloat16 [4096, 2048], P(('dp', 'expert', 'tensor')), may hold values from -3 to 3
- routes: int32 [4096, 2], P(('dp', 'expert', 'tensor')), may hold values from 0 to 7, all different within a row; in each aligned block of 16 rows (0 to 15, 16 to 31, ...) at most 5 rows name the same one
- weight_codes: int32 [4096, 2], P(('dp', 'expert', 'tensor')), may hold values from 16 to 256
- dense_gate: bfloat16 [2048, 8192], P('expert', ('dp', 'tensor')), may hold values from -0.125 to 0.125
- dense_up: bfloat16 [2048, 8192], P('expert', ('dp', 'tensor')), may hold values from -0.125 to 0.125
- dense_down_t: bfloat16 [2048, 8192], P('expert', ('dp', 'tensor')), may hold values from -0.0625 to 0.0625
Outputs:
- mixed: bfloat16 [4096, 2048], P(('dp', 'expert', 'tensor'))
- input_grad: bfloat16 [4096, 2048], P(('dp', 'expert', 'tensor'))
- grad_gate: bfloat16 [8, 2048, 8192], P('expert', None, ('dp', 'tensor'))
- grad_up: bfloat16 [8, 2048, 8192], P('expert', None, ('dp', 'tensor'))
- grad_down_t: bfloat16 [8, 2048, 8192], P('expert', None, ('dp', 'tensor'))
Inputs may be any that keep to these rules, and one draw needn't show every extreme that they name: `routes`: each row names two different experts; the rows of one device name each expert at most 5 times.
All inputs are finite; a program needn't handle non-finite values.
Results may differ from a plain program's by a relative error of at most 0.02.
Values may be sent and summed in bfloat16 or wider, within the bound.
No kernel may reach another device: no remote copies, remote signals or barrier semaphores. Data moves between devices by JAX's collectives and lax.ppermute only.
A program may use at most 128 MiB of HBM per device.

v0:
```python
import jax
import jax.numpy as jnp
from jax import lax
from jax.sharding import PartitionSpec as P


def silu_parts(gate_pre):
    sigmoid_val = jax.nn.sigmoid(gate_pre)
    return (gate_pre * sigmoid_val, sigmoid_val * (1.0 + gate_pre * (1.0 - sigmoid_val)))


def contract_rows(left_side, right_side):
    return lax.dot_general(
        left_side, right_side, (((0,), (0,)), ((), ())), preferred_element_type=jnp.float32
    )


def contract_cols(left_side, right_side):
    return lax.dot_general(
        left_side, right_side, (((1,), (1,)), ((), ())), preferred_element_type=jnp.float32
    )


def expert_rows(rows_x, rows_dy, rows_code, gate_cols, up_cols, down_cols):
    gate_pre = jnp.dot(rows_x, gate_cols, preferred_element_type=jnp.float32)
    up_pre = jnp.dot(rows_x, up_cols, preferred_element_type=jnp.float32)
    activation, act_slope = silu_parts(gate_pre)
    hidden = (activation * up_pre).astype(jnp.bfloat16)
    code_scale = rows_code.astype(jnp.float32) / 256.0
    scaled = (code_scale[:, None] * rows_dy.astype(jnp.float32)).astype(jnp.bfloat16)
    hidden_grad = jnp.dot(scaled, down_cols, preferred_element_type=jnp.float32)
    gate_grad = (hidden_grad * up_pre * act_slope).astype(jnp.bfloat16)
    up_grad = (hidden_grad * activation).astype(jnp.bfloat16)
    weight_grads = (
        contract_rows(rows_x, gate_grad),
        contract_rows(rows_x, up_grad),
        contract_rows(scaled, hidden),
    )
    return (hidden, gate_grad, up_grad, weight_grads)


def shards(tokens, cotangent, routes, weight_codes, dense_gate, dense_up, dense_down_t):
    gate_cols, up_cols, down_cols = (
        lax.all_gather(dense_gate, "expert", axis=0, tiled=True),
        lax.all_gather(dense_up, "expert", axis=0, tiled=True),
        lax.all_gather(dense_down_t, "expert", axis=0, tiled=True),
    )
    experts = lax.axis_size("expert")
    count_tok, model_width = tokens.shape
    capacity = 5 * count_tok // (2 * experts)
    slots_here = experts * capacity
    flat_route = routes.reshape(-1)
    flat_code = weight_codes.reshape(-1)
    onehot = (flat_route[:, None] == jnp.arange(experts, dtype=jnp.int32)[None, :]).astype(
        jnp.int32
    )
    earlier = jnp.cumsum(onehot, axis=0) - onehot
    slot_of = flat_route * capacity + jnp.sum(earlier * onehot, axis=1)
    placed = (slot_of[None, :] == jnp.arange(slots_here, dtype=jnp.int32)[:, None]).astype(
        jnp.int32
    )
    placed_tok = placed.reshape(slots_here, count_tok, 2).sum(axis=2)
    place_table = placed_tok.astype(jnp.bfloat16)
    send_x = jnp.dot(place_table, tokens, preferred_element_type=jnp.float32).astype(jnp.bfloat16)
    send_dy = jnp.dot(place_table, cotangent, preferred_element_type=jnp.float32).astype(
        jnp.bfloat16
    )
    send_code = jnp.sum(placed * flat_code[None, :], axis=1)
    parcel = (
        lax.all_to_all(
            send_x.reshape(experts, capacity, model_width),
            "expert",
            split_axis=0,
            concat_axis=0,
            tiled=True,
        ),
        lax.all_to_all(
            send_dy.reshape(experts, capacity, model_width),
            "expert",
            split_axis=0,
            concat_axis=0,
            tiled=True,
        ),
        lax.all_to_all(
            send_code.reshape(experts, capacity), "expert", split_axis=0, concat_axis=0, tiled=True
        ),
    )
    parcel = (
        lax.all_gather(parcel[0], ("dp", "tensor"), axis=0, tiled=True),
        lax.all_gather(parcel[1], ("dp", "tensor"), axis=0, tiled=True),
        lax.all_gather(parcel[2], ("dp", "tensor"), axis=0, tiled=True),
    )
    all_x = parcel[0].reshape(-1, model_width)
    all_dy = parcel[1].reshape(-1, model_width)
    all_code = parcel[2].reshape(-1)
    hidden, gate_grad, up_grad, weight_grads = expert_rows(
        all_x, all_dy, all_code, gate_cols, up_cols, down_cols
    )
    out_rows = lax.psum_scatter(
        contract_cols(hidden, down_cols).astype(jnp.bfloat16),
        ("dp", "tensor"),
        scatter_dimension=0,
        tiled=True,
    )
    grad_rows = lax.psum_scatter(
        (contract_cols(gate_grad, gate_cols) + contract_cols(up_grad, up_cols)).astype(
            jnp.bfloat16
        ),
        ("dp", "tensor"),
        scatter_dimension=0,
        tiled=True,
    )
    back_out, back_grad = (
        lax.all_to_all(
            out_rows.reshape(experts, capacity, model_width),
            "expert",
            split_axis=0,
            concat_axis=0,
            tiled=True,
        ),
        lax.all_to_all(
            grad_rows.reshape(experts, capacity, model_width),
            "expert",
            split_axis=0,
            concat_axis=0,
            tiled=True,
        ),
    )
    code_scale = flat_code.astype(jnp.float32) / 256.0
    weighted = (
        (placed.astype(jnp.float32) * code_scale[None, :])
        .reshape(slots_here, count_tok, 2)
        .sum(axis=2)
    )
    mixed = lax.dot_general(
        weighted,
        back_out.reshape(slots_here, model_width).astype(jnp.float32),
        (((0,), (0,)), ((), ())),
        precision=lax.Precision.HIGHEST,
        preferred_element_type=jnp.float32,
    ).astype(jnp.bfloat16)
    input_grad = contract_rows(place_table, back_grad.reshape(slots_here, model_width)).astype(
        jnp.bfloat16
    )
    grad_gate = weight_grads[0].astype(jnp.bfloat16)[None]
    grad_up = weight_grads[1].astype(jnp.bfloat16)[None]
    grad_down_t = weight_grads[2].astype(jnp.bfloat16)[None]
    return (mixed, input_grad, grad_gate, grad_up, grad_down_t)


def solution(mesh):
    placed = (
        P(("dp", "expert", "tensor"), None),
        P(("dp", "expert", "tensor"), None),
        P(("dp", "expert", "tensor"), None),
        P(("dp", "expert", "tensor"), None),
        P("expert", ("dp", "tensor")),
        P("expert", ("dp", "tensor")),
        P("expert", ("dp", "tensor")),
    )
    return jax.shard_map(
        shards,
        mesh=mesh,
        in_specs=placed,
        out_specs=(
            P(("dp", "expert", "tensor"), None),
            P(("dp", "expert", "tensor"), None),
            P("expert", None, ("dp", "tensor")),
            P("expert", None, ("dp", "tensor")),
            P("expert", None, ("dp", "tensor")),
        ),
        check_vma=False,
    )
```

profile of v0, /device:TPU:2, one launch (start us, length us, event | category | flops | bytes accessed | tf_op | source)
XLA Modules:
  0.0 478.8 jit_solution(12512945700379093156)
XLA Ops:
  7.2 0.8 copy.52
  8.2 0.2 select_reduce_fusion.1
  8.5 0.1 copy.53
  8.6 0.7 multiply_add_fusion
  9.3 0.2 convolution_convert_fusion.5
  9.6 20.1 %all_to_all.32 = bf16[8,5,2048]{2,1,0:T(8,128)(2,1)S(1)} all-to-all(bf16[8,5,2048]{2,1,0:T(8,128)(2,1)S(1)} %reshape.89), channel_id=1, replica_groups=mesh['dp'=8,'expert'=8,'tensor'=4] {'expert'}, dimensions={0} | all-to-all | bytes 327680 | tf_op jit(solution)/shard_map/all_to_all | solution.py:70
  29.8 0.8 copy.54
  30.6 1.1 convolution_convert_fusion.4
  31.8 12.9 %all_to_all.33 = bf16[8,5,2048]{2,1,0:T(8,128)(2,1)S(1)} all-to-all(bf16[8,5,2048]{2,1,0:T(8,128)(2,1)S(1)} %reshape.93), channel_id=1, replica_groups=mesh['dp'=8,'expert'=8,'tensor'=4] {'expert'}, dimensions={0} | all-to-all | bytes 327680 | tf_op jit(solution)/shard_map/all_to_all | solution.py:77
  44.7 0.8 copy.58
  45.6 0.7 all-gather.9.cloned.1.call-update
  46.3 0.5 all-gather.11.cloned.1.call-update
  46.9 0.5 all-gather.13.cloned.1.call-update
  47.5 0.8 copy.56
  48.3 0.1 select_reduce_fusion
  48.5 10.0 %all_to_all.34 = s32[8,1,5]{2,1,0:T(1,128)S(1)} all-to-all(s32[8,1,5]{2,1,0:T(1,128)S(1)} %bitcast.28), channel_id=1, replica_groups=mesh['dp'=8,'expert'=8,'tensor'=4] {'expert'}, dimensions={0} | all-to-all | bytes 320 | tf_op jit(solution)/shard_map/all_to_all | solution.py:84
  58.5 24.6 %all-gather = s32[256,1,5]{2,1,0:T(1,128)S(1)} all-gather(s32[8,1,5]{2,1,0:T(1,128)S(1)} %all_to_all.34), channel_id=2, replica_groups=mesh['dp'=8,'expert'=8,'tensor'=4] {'dp','tensor'}, dimensions={0}, use_global_device_ids=true | all-gather | bytes 5280 | tf_op jit(solution)/shard_map/all_gather | solution.py:91
  83.1 0.4 multiply_reduce_fusion
  83.5 0.2 div.22
  83.7 8.9 %copy.55 = bf16[256,5,2048]{2,1,0:T(8,128)(2,1)} copy(bf16[256,5,2048]{2,0,1:T(8,128)(2,1)} %all-gather.7.cloned.1.call-done) | data formatting | bytes 10485760 | tf_op jit(solution)/shard_map/all_gather | solution.py:89
  92.7 10.0 %reshape.90 = bf16[1280,2048]{1,0:T(8,128)(2,1)} reshape(bf16[256,5,2048]{2,1,0:T(8,128)(2,1)} %copy.55) | data formatting | bytes 10485760 | tf_op jit(solution)/shard_map/reshape | solution.py:93
  102.7 31.9 %all-gather.15.cloned.1.call-done = bf16[256,5,2048]{2,0,1:T(8,128)(2,1)} async-done(((bf16[8,5,2048]{2,0,1:T(8,128)(2,1)}), bf16[256,5,2048]{2,0,1:T(8,128)(2,1)}) %all-gather.15.cloned.1.call-update) | async-done | bytes 5242896 | tf_op jit(solution)/shard_map/all_gather | solution.py:90
  134.6 11.5 %copy.59 = f32[256,5,2048]{2,1,0:T(8,128)} copy(bf16[256,5,2048]{2,0,1:T(8,128)(2,1)} %all-gather.15.cloned.1.call-done) | data formatting | bytes 15728640 | tf_op jit(solution)/shard_map/convert_element_type | solution.py:30
  146.1 14.1 %reshape.96 = f32[1280,2048]{1,0:T(8,128)} reshape(f32[256,5,2048]{2,1,0:T(8,128)} %copy.59) | data formatting | bytes 20971520 | tf_op jit(solution)/shard_map/convert_element_type | solution.py:30
  160.2 14.7 %all-gather.9.cloned.1.call-done = bf16[2048,256]{1,0:T(8,128)(2,1)} async-done(((bf16[256,256]{1,0:T(8,128)(2,1)}), bf16[2048,256]{1,0:T(8,128)(2,1)}) %all-gather.9.cloned.1.call-update) | async-done | bytes 1048592 | tf_op jit(solution)/shard_map/all_gather | solution.py:44
  174.9 5.4 %fusion.11 = f32[1280,256]{1,0:T(8,128)} fusion(bf16[1280,2048]{1,0:T(8,128)(2,1)} %reshape.90, bf16[2048,256]{1,0:T(8,128)(2,1)} %all-gather.9.cloned.1.call-done), kind=kOutput, calls=%fused_computation.36 | convolution fusion | flops 1342177280 | bytes 7602176 | tf_op jit(solution)/shard_map/dot_general | solution.py:25
  180.3 33.5 %all-gather.11.cloned.1.call-done = bf16[2048,256]{1,0:T(8,128)(2,1)} async-done(((bf16[256,256]{1,0:T(8,128)(2,1)}), bf16[2048,256]{1,0:T(8,128)(2,1)}) %all-gather.11.cloned.1.call-update) | async-done | bytes 1048592 | tf_op jit(solution)/shard_map/all_gather | solution.py:45
  213.8 5.4 %fusion.12 = f32[1280,256]{1,0:T(8,128)} fusion(bf16[1280,2048]{1,0:T(8,128)(2,1)} %reshape.90, bf16[2048,256]{1,0:T(8,128)(2,1)} %all-gather.11.cloned.1.call-done), kind=kOutput, calls=%fused_computation.37 | convolution fusion | flops 1342177280 | bytes 7602176 | tf_op jit(solution)/shard_map/dot_general | solution.py:26
  219.1 33.5 %all-gather.13.cloned.1.call-done = bf16[2048,256]{1,0:T(8,128)(2,1)} async-done(((bf16[256,256]{1,0:T(8,128)(2,1)}), bf16[2048,256]{1,0:T(8,128)(2,1)}) %all-gather.13.cloned.1.call-update) | async-done | bytes 1048592 | tf_op jit(solution)/shard_map/all_gather | solution.py:46
  252.6 7.0 %multiply_convert_fusion.1 = (bf16[1280,256]{1,0:T(8,128)(2,1)S(1)}, bf16[1280,256]{1,0:T(8,128)(2,1)S(1)}, bf16[1280,256]{1,0:T(8,128)(2,1)S(1)}) fusion(f32[1280,256]{1,0:T(8,128)} %fusion.11, f32[1280,256]{1,0:T(8,128)} %fusion.12, bf16[2048,256]{1,0:T(8,128)(2,1)} %all-gather.13.cloned.1.call-done, f32[1280,2048]{1,0:T(8,128)} %reshape.96, ...), kind=kOutput, calls=%fused_computation.13 | convolution fusion | flops 1352335360 | bytes 16126976 | tf_op jit(solution)/shard_map/dot_general | solution.py:31
  259.7 1.6 fusion.13
  261.3 3.9 add_convert_fusion
  265.2 0.3 reduce-scatter.3.cloned.1.call-start
  265.4 0.9 copy-done.3
  266.4 3.9 convolution_convert_fusion
  270.3 0.7 copy-done.5
  271.0 6.9 %fusion.2 = bf16[1,2048,256]{2,1,0:T(8,128)(2,1)} fusion(bf16[1280,256]{1,0:T(8,128)(2,1)S(1)} %get-tuple-element.7, f32[1280,2048]{1,0:T(8,128)} %reshape.96, f32[1280]{0:T(1024)S(1)} %div.22), kind=kOutput, calls=%fused_computation.8 | convolution fusion | flops 1347944448 | bytes 12194816 | tf_op jit(solution)/shard_map/dot_general | solution.py:13
  277.9 77.7 %reduce-scatter.5.cloned.1.call-done = bf16[40,2048]{1,0:T(8,128)(2,1)} async-done(((bf16[1280,2048]{1,0:T(8,128)(2,1)}), bf16[40,2048]{1,0:T(8,128)(2,1)}) %reduce-scatter.5.cloned.1.call-update) | async-done | bytes 163856 | tf_op jit(solution)/shard_map/reduce_scatter | solution.py:105
  355.7 1.7 reshape.94
  357.4 7.0 %all-to-all-start.4 = ((bf16[8,5,2048]{2,1,0:T(8,128)(2,1)}), bf16[8,5,2048]{2,1,0:T(8,128)(2,1)S(1)}, u32[]{:S(2)}, u32[]{:S(2)}) async-start(bf16[8,5,2048]{2,1,0:T(8,128)(2,1)} %reshape.94), calls=%async_computation.6 | async-start | bytes 524288 | tf_op jit(solution)/shard_map/all_to_all | solution.py:121
  364.4 5.1 %fusion = bf16[1,2048,256]{2,1,0:T(8,128)(2,1)} fusion(bf16[1280,2048]{1,0:T(8,128)(2,1)} %reshape.90, bf16[1280,256]{1,0:T(8,128)(2,1)S(1)} %get-tuple-element.6), kind=kOutput, calls=%fused_computation.6 | convolution fusion | flops 1342701568 | bytes 6946816 | tf_op jit(solution)/shard_map/dot_general | solution.py:13
  369.5 82.4 %reduce-scatter.3.cloned.1.call-done = bf16[40,2048]{1,0:T(8,128)(2,1)} async-done(((bf16[1280,2048]{1,0:T(8,128)(2,1)}), bf16[40,2048]{1,0:T(8,128)(2,1)}) %reduce-scatter.3.cloned.1.call-update) | async-done | bytes 163856 | tf_op jit(solution)/shard_map/reduce_scatter | solution.py:99
  451.8 1.7 reshape.91
  453.5 7.0 %all-to-all-start.1 = ((bf16[8,5,2048]{2,1,0:T(8,128)(2,1)}), bf16[8,5,2048]{2,1,0:T(8,128)(2,1)S(1)}, u32[]{:S(2)}, u32[]{:S(2)}) async-start(bf16[8,5,2048]{2,1,0:T(8,128)(2,1)} %reshape.91), calls=%async_computation.2 | async-start | bytes 524288 | tf_op jit(solution)/shard_map/all_to_all | solution.py:114
  460.5 5.1 %fusion.1 = bf16[1,2048,256]{2,1,0:T(8,128)(2,1)} fusion(bf16[1280,2048]{1,0:T(8,128)(2,1)} %reshape.90, bf16[1280,256]{1,0:T(8,128)(2,1)S(1)} %get-tuple-element.5), kind=kOutput, calls=%fused_computation.7 | convolution fusion | flops 1342701568 | bytes 6946816 | tf_op jit(solution)/shard_map/dot_general | solution.py:13
  465.7 0.8 convolution_convert_fusion.6
  466.5 4.5 all-to-all-done.1
  471.1 0.8 convolution_convert_fusion.7
  (36 shorter events, 1.3 us)
Async XLA Ops:
  7.2 2.2 copy-start
  7.2 76.6 %all-gather.7.cloned.1.call-start = ((), (), s32[]{:S(2)}) async-start(), calls=%async_computation.7 | async-start | bytes 5406720 | tf_op jit(solution)/shard_map/all_gather | solution.py:89
  30.6 104.0 %all-gather.15.cloned.1.call-start = ((), (), s32[]{:S(2)}) async-start(), calls=%async_computation.12 | async-start | bytes 5406720 | tf_op jit(solution)/shard_map/all_gather | solution.py:90
  45.5 129.4 %all-gather.9.cloned.1.call-start = ((), (), s32[]{:S(2)}) async-start(), calls=%async_computation.8 | async-start | bytes 1179648 | tf_op jit(solution)/shard_map/all_gather | solution.py:44
  46.3 167.5 %all-gather.11.cloned.1.call-start = ((), (), s32[]{:S(2)}) async-start(), calls=%async_computation.9 | async-start | bytes 1179648 | tf_op jit(solution)/shard_map/all_gather | solution.py:45
  46.8 205.8 %all-gather.13.cloned.1.call-start = ((), (), s32[]{:S(2)}) async-start(), calls=%async_computation.10 | async-start | bytes 1179648 | tf_op jit(solution)/shard_map/all_gather | solution.py:46
  47.4 308.3 %reduce-scatter.5.cloned.1.call-start = ((), (), s32[]{:S(2)}) async-start(), calls=%async_computation.13 | async-start | bytes 5406720 | tf_op jit(solution)/shard_map/reduce_scatter | solution.py:105
  219.1 40.6 %copy-start.2 = (bf16[2048,256]{1,0:T(8,128)(2,1)S(1)}, bf16[2048,256]{1,0:T(8,128)(2,1)}, u32[]{:S(2)}) copy-start(bf16[2048,256]{1,0:T(8,128)(2,1)} %all-gather.9.cloned.1.call-done) | copy-start | bytes 3145732
  259.7 1.6 copy-start.4
  265.1 1.2 copy-start.3
  265.2 186.7 %reduce-scatter.3.cloned.1.call-start = ((), (), s32[]{:S(2)}) async-start(), calls=%async_computation.11 | async-start | bytes 5406720 | tf_op jit(solution)/shard_map/reduce_scatter | solution.py:99
  270.3 0.7 copy-start.5
  357.4 96.1 %all-to-all-start.4 = ((bf16[8,5,2048]{2,1,0:T(8,128)(2,1)}), bf16[8,5,2048]{2,1,0:T(8,128)(2,1)S(1)}, u32[]{:S(2)}, u32[]{:S(2)}) async-start(bf16[8,5,2048]{2,1,0:T(8,128)(2,1)} %reshape.94), calls=%async_computation.6 | async-start | bytes 524288 | tf_op jit(solution)/shard_map/all_to_all | solution.py:121
  453.5 17.5 %all-to-all-start.1 = ((bf16[8,5,2048]{2,1,0:T(8,128)(2,1)}), bf16[8,5,2048]{2,1,0:T(8,128)(2,1)S(1)}, u32[]{:S(2)}, u32[]{:S(2)}) async-start(bf16[8,5,2048]{2,1,0:T(8,128)(2,1)} %reshape.91), calls=%async_computation.2 | async-start | bytes 524288 | tf_op jit(solution)/shard_map/all_to_all | solution.py:114
  460.5 11.4 %copy-start.1 = (bf16[16,2048]{1,0:T(8,128)(2,1)S(1)}, bf16[16,2048]{1,0:T(8,128)(2,1)}, u32[]{:S(2)}) copy-start(bf16[16,2048]{1,0:T(8,128)(2,1)} %param.7) | copy-start | bytes 196612
Sparse Core Ops, SparseCore 0:
  30.7 48.5 all-gather.6
  82.5 52.0 all-gather.14
  136.4 38.4 all-gather.8
  176.5 37.1 all-gather.10
  215.4 37.1 all-gather.12
  265.3 90.3 reduce-scatter.4
  360.2 91.5 reduce-scatter.2
where the time goes:
time: 480 us; the launch traced here: 479 us
  waiting for transfers between devices  280 us (58%)
  blocking collectives  67.7 us (14%)
  local copies, waits for them, and re-layouts  53.5 us (11%)
  matrix products  47.1 us (10%)
  starting transfers between devices  14.6 us (3%)
  between operations  14.3 us (3%)
    reduce_scatter x1, waiting for transfers between devices, shards(): lax.psum_scatter(contract_cols(hidden, down_cols).astype(jnp.bfloat16), (...  82.4 us
    reduce_scatter x1, waiting for transfers between devices, shards(): lax.psum_scatter((contract_cols(gate_grad, gate_cols) + contract_cols(up_...  77.7 us
    all_gather x1, waiting for transfers between devices, shards(): lax.all_gather(dense_down_t, 'expert', axis=0, tiled=True)  33.5 us
    all_gather x1, waiting for transfers between devices, shards(): lax.all_gather(dense_up, 'expert', axis=0, tiled=True)  33.5 us
    all_gather x1, waiting for transfers between devices, shards(): lax.all_gather(parcel[1], ('dp', 'tensor'), axis=0, tiled=True)  31.9 us
    convert_element_type x2, local copies, waits for them, and re-layouts, expert_rows(): rows_dy.astype(jnp.float32)  25.6 us
    all_gather x1, blocking collectives, shards(): lax.all_gather(parcel[2], ('dp', 'tensor'), axis=0, tiled=True)  24.6 us
    all_to_all x1, blocking collectives, shards(): lax.all_to_all(send_x.reshape(experts, capacity, model_width), 'expert',...  20.1 us
  transfers between devices with their start and end apart: 9, of which 7 were waited for; matrix products, arithmetic and copies ran while one was open for 18% of the time, Pallas kernels for 0%

commit v1 on v0

--- a/solution.py
+++ b/solution.py
@@ -2,6 +2,18 @@
 import jax.numpy as jnp
 from jax import lax
 from jax.sharding import PartitionSpec as P
+
+
+def wait_waves_on_mesh(panel):
+    return jnp.concatenate(
+        lax.all_to_all(
+            jnp.stack(tuple((panel for _ in range(lax.axis_size("expert")))), axis=0),
+            "expert",
+            0,
+            0,
+        ),
+        axis=0,
+    )
 
 
 def silu_parts(gate_pre):
@@ -41,7 +53,7 @@
 
 def shards(tokens, cotangent, routes, weight_codes, dense_gate, dense_up, dense_down_t):
     gate_cols, up_cols, down_cols = (
-        lax.all_gather(dense_gate, "expert", axis=0, tiled=True),
+        wait_waves_on_mesh(dense_gate),
         lax.all_gather(dense_up, "expert", axis=0, tiled=True),
         lax.all_gather(dense_down_t, "expert", axis=0, tiled=True),
     )

time: 480 us -> 441 us (0.919)
  waiting for transfers between devices: 280 us -> 236 us
    all_gather x1, waiting for transfers between devices: 33.5 us -> 9.62 us  [shards(): lax.all_gather(dense_up, 'expert', axis=0, tiled=True)]
    all_gather x1 -> x0, waiting for transfers between devices: 14.7 us -> none  [shards(): lax.all_gather(dense_gate, 'expert', axis=0, tiled=True)]
    all_gather x1, waiting for transfers between devices: 31.9 us -> 26.9 us  [shards(): lax.all_gather(parcel[1], ('dp', 'tensor'), axis=0, tiled=True)]
  transfers between devices with their start and end apart: 9 -> 9, of which waited for: 7 -> 6; matrix products, arithmetic and copies ran while one was open for 18% -> 19% of each run, Pallas kernels for 0% -> 0%
where the time goes in v1:
time: 441 us; the launch traced here: 440 us
  waiting for transfers between devices  236 us (54%)
  blocking collectives  67.7 us (15%)
  local copies, waits for them, and re-layouts  55.4 us (13%)
  matrix products  46.8 us (11%)
  starting transfers between devices  18.1 us (4%)
  between operations  14.2 us (3%)
    reduce_scatter x1, waiting for transfers between devices, shards(): lax.psum_scatter(contract_cols(hidden, down_cols).astype(jnp.bfloat16), (...  82.3 us
    reduce_scatter x1, waiting for transfers between devices, shards(): lax.psum_scatter((contract_cols(gate_grad, gate_cols) + contract_cols(up_...  77.7 us
    all_gather x1, waiting for transfers between devices, shards(): lax.all_gather(dense_down_t, 'expert', axis=0, tiled=True)  33.5 us
    all_gather x1, waiting for transfers between devices, shards(): lax.all_gather(parcel[1], ('dp', 'tensor'), axis=0, tiled=True)  26.9 us
    convert_element_type x2, local copies, waits for them, and re-layouts, expert_rows(): rows_dy.astype(jnp.float32)  25.6 us
    all_gather x1, blocking collectives, shards(): lax.all_gather(parcel[2], ('dp', 'tensor'), axis=0, tiled=True)  24.6 us
    all_to_all x1, blocking collectives, shards(): lax.all_to_all(send_x.reshape(experts, capacity, model_width), 'expert',...  20.1 us
    dot_general x4, matrix products, contract_rows(): lax.dot_general(left_side, right_side, (((0,), (0,)), ((), ())), preferre...  17.9 us
  transfers between devices with their start and end apart: 9, of which 6 were waited for; matrix products, arithmetic and copies ran while one was open for 19% of the time, Pallas kernels for 0%

profile of v1, /device:TPU:2, one launch (start us, length us, event | category | flops | bytes accessed | tf_op | source)
XLA Modules:
  0.0 439.8 jit_solution(5025979527332592818)
XLA Ops:
  7.2 0.8 copy.52
  8.2 0.2 select_reduce_fusion.1
  8.5 0.1 copy.53
  8.6 0.7 multiply_add_fusion
  9.3 0.2 convolution_convert_fusion.5
  9.6 20.1 %all_to_all.37 = bf16[8,5,2048]{2,1,0:T(8,128)(2,1)S(1)} all-to-all(bf16[8,5,2048]{2,1,0:T(8,128)(2,1)S(1)} %reshape.94), channel_id=1, replica_groups=mesh['dp'=8,'expert'=8,'tensor'=4] {'expert'}, dimensions={0} | all-to-all | bytes 327680 | tf_op jit(solution)/shard_map/all_to_all | solution.py:82
  29.8 0.8 copy.54
  30.6 1.1 convolution_convert_fusion.4
  31.8 12.9 %all_to_all.38 = bf16[8,5,2048]{2,1,0:T(8,128)(2,1)S(1)} all-to-all(bf16[8,5,2048]{2,1,0:T(8,128)(2,1)S(1)} %reshape.99), channel_id=1, replica_groups=mesh['dp'=8,'expert'=8,'tensor'=4] {'expert'}, dimensions={0} | all-to-all | bytes 327680 | tf_op jit(solution)/shard_map/all_to_all | solution.py:89
  44.7 0.8 copy.58
  45.6 0.7 all-gather.8.cloned.1.call-update
  46.3 0.8 copy.56
  47.1 0.1 select_reduce_fusion
  47.3 10.0 %all_to_all.39 = s32[8,1,5]{2,1,0:T(1,128)S(1)} all-to-all(s32[8,1,5]{2,1,0:T(1,128)S(1)} %bitcast.31), channel_id=1, replica_groups=mesh['dp'=8,'expert'=8,'tensor'=4] {'expert'}, dimensions={0} | all-to-all | bytes 320 | tf_op jit(solution)/shard_map/all_to_all | solution.py:96
  57.3 1.9 stack.2
  59.3 3.6 all-to-all-start.1
  62.9 0.5 all-gather.10.cloned.1.call-update
  63.5 24.6 %all-gather = s32[256,1,5]{2,1,0:T(1,128)S(1)} all-gather(s32[8,1,5]{2,1,0:T(1,128)S(1)} %all_to_all.39), channel_id=2, replica_groups=mesh['dp'=8,'expert'=8,'tensor'=4] {'dp','tensor'}, dimensions={0}, use_global_device_ids=true | all-gather | bytes 5280 | tf_op jit(solution)/shard_map/all_gather | solution.py:103
  88.1 0.4 multiply_reduce_fusion
  88.5 0.2 div.22
  88.7 8.9 %copy.55 = bf16[256,5,2048]{2,1,0:T(8,128)(2,1)} copy(bf16[256,5,2048]{2,0,1:T(8,128)(2,1)} %all-gather.6.cloned.1.call-done) | data formatting | bytes 10485760 | tf_op jit(solution)/shard_map/all_gather | solution.py:101
  97.6 10.0 %reshape.95 = bf16[1280,2048]{1,0:T(8,128)(2,1)} reshape(bf16[256,5,2048]{2,1,0:T(8,128)(2,1)} %copy.55) | data formatting | bytes 10485760 | tf_op jit(solution)/shard_map/reshape | solution.py:105
  107.6 26.9 %all-gather.12.cloned.1.call-done = bf16[256,5,2048]{2,0,1:T(8,128)(2,1)} async-done(((bf16[8,5,2048]{2,0,1:T(8,128)(2,1)}), bf16[256,5,2048]{2,0,1:T(8,128)(2,1)}) %all-gather.12.cloned.1.call-update) | async-done | bytes 5242896 | tf_op jit(solution)/shard_map/all_gather | solution.py:102
  134.6 11.5 %copy.59 = f32[256,5,2048]{2,1,0:T(8,128)} copy(bf16[256,5,2048]{2,0,1:T(8,128)(2,1)} %all-gather.12.cloned.1.call-done) | data formatting | bytes 15728640 | tf_op jit(solution)/shard_map/convert_element_type | solution.py:42
  146.0 14.1 %reshape.102 = f32[1280,2048]{1,0:T(8,128)} reshape(f32[256,5,2048]{2,1,0:T(8,128)} %copy.59) | data formatting | bytes 20971520 | tf_op jit(solution)/shard_map/convert_element_type | solution.py:42
  160.1 5.1 %fusion.11 = f32[1280,256]{1,0:T(8,128)} fusion(bf16[1280,2048]{1,0:T(8,128)(2,1)} %reshape.95, bf16[2048,256]{1,0:T(8,128)(2,1)S(1)} %bitcast.29), kind=kOutput, calls=%fused_computation.36 | convolution fusion | flops 1342177280 | bytes 7602176 | tf_op jit(solution)/shard_map/dot_general | solution.py:37
  165.2 9.6 %all-gather.8.cloned.1.call-done = bf16[2048,256]{1,0:T(8,128)(2,1)} async-done(((bf16[256,256]{1,0:T(8,128)(2,1)}), bf16[2048,256]{1,0:T(8,128)(2,1)}) %all-gather.8.cloned.1.call-update) | async-done | bytes 1048592 | tf_op jit(solution)/shard_map/all_gather | solution.py:57
  174.9 5.4 %fusion.12 = f32[1280,256]{1,0:T(8,128)} fusion(bf16[1280,2048]{1,0:T(8,128)(2,1)} %reshape.95, bf16[2048,256]{1,0:T(8,128)(2,1)} %all-gather.8.cloned.1.call-done), kind=kOutput, calls=%fused_computation.37 | convolution fusion | flops 1342177280 | bytes 7602176 | tf_op jit(solution)/shard_map/dot_general | solution.py:38
  180.2 33.5 %all-gather.10.cloned.1.call-done = bf16[2048,256]{1,0:T(8,128)(2,1)} async-done(((bf16[256,256]{1,0:T(8,128)(2,1)}), bf16[2048,256]{1,0:T(8,128)(2,1)}) %all-gather.10.cloned.1.call-update) | async-done | bytes 1048592 | tf_op jit(solution)/shard_map/all_gather | solution.py:58
  213.7 7.0 %multiply_convert_fusion.1 = (bf16[1280,256]{1,0:T(8,128)(2,1)S(1)}, bf16[1280,256]{1,0:T(8,128)(2,1)S(1)}, bf16[1280,256]{1,0:T(8,128)(2,1)S(1)}) fusion(f32[1280,256]{1,0:T(8,128)} %fusion.11, f32[1280,256]{1,0:T(8,128)} %fusion.12, bf16[2048,256]{1,0:T(8,128)(2,1)} %all-gather.10.cloned.1.call-done, f32[1280,2048]{1,0:T(8,128)} %reshape.102, ...), kind=kOutput, calls=%fused_computation.13 | convolution fusion | flops 1352335360 | bytes 16126976 | tf_op jit(solution)/shard_map/dot_general | solution.py:43
  220.8 1.6 fusion.13
  222.4 3.9 add_convert_fusion
  226.3 0.3 reduce-scatter.3.cloned.1.call-start
  226.6 0.9 copy-done.3
  227.5 3.9 convolution_convert_fusion
  231.4 0.7 copy-done.4
  232.1 6.9 %fusion.2 = bf16[1,2048,256]{2,1,0:T(8,128)(2,1)} fusion(bf16[1280,256]{1,0:T(8,128)(2,1)S(1)} %get-tuple-element.7, f32[1280,2048]{1,0:T(8,128)} %reshape.102, f32[1280]{0:T(1024)S(1)} %div.22), kind=kOutput, calls=%fused_computation.8 | convolution fusion | flops 1347944448 | bytes 12194816 | tf_op jit(solution)/shard_map/dot_general | solution.py:25
  239.1 77.7 %reduce-scatter.5.cloned.1.call-done = bf16[40,2048]{1,0:T(8,128)(2,1)} async-done(((bf16[1280,2048]{1,0:T(8,128)(2,1)}), bf16[40,2048]{1,0:T(8,128)(2,1)}) %reduce-scatter.5.cloned.1.call-update) | async-done | bytes 163856 | tf_op jit(solution)/shard_map/reduce_scatter | solution.py:117
  316.7 1.7 reshape.100
  318.4 7.0 %all-to-all-start.5 = ((bf16[8,5,2048]{2,1,0:T(8,128)(2,1)}), bf16[8,5,2048]{2,1,0:T(8,128)(2,1)S(1)}, u32[]{:S(2)}, u32[]{:S(2)}) async-start(bf16[8,5,2048]{2,1,0:T(8,128)(2,1)} %reshape.100), calls=%async_computation.7 | async-start | bytes 524288 | tf_op jit(solution)/shard_map/all_to_all | solution.py:133
  325.5 5.1 %fusion = bf16[1,2048,256]{2,1,0:T(8,128)(2,1)} fusion(bf16[1280,2048]{1,0:T(8,128)(2,1)} %reshape.95, bf16[1280,256]{1,0:T(8,128)(2,1)S(1)} %get-tuple-element.6), kind=kOutput, calls=%fused_computation.6 | convolution fusion | flops 1342701568 | bytes 6946816 | tf_op jit(solution)/shard_map/dot_general | solution.py:25
  330.5 82.3 %reduce-scatter.3.cloned.1.call-done = bf16[40,2048]{1,0:T(8,128)(2,1)} async-done(((bf16[1280,2048]{1,0:T(8,128)(2,1)}), bf16[40,2048]{1,0:T(8,128)(2,1)}) %reduce-scatter.3.cloned.1.call-update) | async-done | bytes 163856 | tf_op jit(solution)/shard_map/reduce_scatter | solution.py:111
  412.8 1.7 reshape.97
  414.5 7.0 %all-to-all-start.2 = ((bf16[8,5,2048]{2,1,0:T(8,128)(2,1)}), bf16[8,5,2048]{2,1,0:T(8,128)(2,1)S(1)}, u32[]{:S(2)}, u32[]{:S(2)}) async-start(bf16[8,5,2048]{2,1,0:T(8,128)(2,1)} %reshape.97), calls=%async_computation.3 | async-start | bytes 524288 | tf_op jit(solution)/shard_map/all_to_all | solution.py:126
  421.5 5.1 %fusion.1 = bf16[1,2048,256]{2,1,0:T(8,128)(2,1)} fusion(bf16[1280,2048]{1,0:T(8,128)(2,1)} %reshape.95, bf16[1280,256]{1,0:T(8,128)(2,1)S(1)} %get-tuple-element.5), kind=kOutput, calls=%fused_computation.7 | convolution fusion | flops 1342701568 | bytes 6946816 | tf_op jit(solution)/shard_map/dot_general | solution.py:25
  426.7 0.8 convolution_convert_fusion.6
  427.5 4.5 %all-to-all-done.2 = bf16[8,5,2048]{2,1,0:T(8,128)(2,1)S(1)} async-done(((bf16[8,5,2048]{2,1,0:T(8,128)(2,1)}), bf16[8,5,2048]{2,1,0:T(8,128)(2,1)S(1)}, u32[]{:S(2)}, u32[]{:S(2)}) %all-to-all-start.2) | async-done | bytes 163872 | tf_op jit(solution)/shard_map/all_to_all | solution.py:126
  432.1 0.8 convolution_convert_fusion.7
  (34 shorter events, 1.2 us)
Async XLA Ops:
  7.2 2.2 copy-start
  7.2 81.5 %all-gather.6.cloned.1.call-start = ((), (), s32[]{:S(2)}) async-start(), calls=%async_computation.8 | async-start | bytes 5406720 | tf_op jit(solution)/shard_map/all_gather | solution.py:101
  30.6 104.0 %all-gather.12.cloned.1.call-start = ((), (), s32[]{:S(2)}) async-start(), calls=%async_computation.12 | async-start | bytes 5406720 | tf_op jit(solution)/shard_map/all_gather | solution.py:102
  45.5 129.3 %all-gather.8.cloned.1.call-start = ((), (), s32[]{:S(2)}) async-start(), calls=%async_computation.9 | async-start | bytes 1179648 | tf_op jit(solution)/shard_map/all_gather | solution.py:57
  59.3 100.9 %all-to-all-start.1 = ((bf16[8,256,256]{2,1,0:T(8,128)(2,1)}), bf16[8,256,256]{2,1,0:T(8,128)(2,1)S(1)}, u32[]{:S(2)}, u32[]{:S(2)}) async-start(bf16[8,256,256]{2,1,0:T(8,128)(2,1)} %stack.2), calls=%async_computation.1 | async-start | bytes 2097152 | tf_op jit(solution)/shard_map/all_to_all | solution.py:9
  62.8 150.9 %all-gather.10.cloned.1.call-start = ((), (), s32[]{:S(2)}) async-start(), calls=%async_computation.10 | async-start | bytes 1179648 | tf_op jit(solution)/shard_map/all_gather | solution.py:58
  63.4 253.3 %reduce-scatter.5.cloned.1.call-start = ((), (), s32[]{:S(2)}) async-start(), calls=%async_computation.13 | async-start | bytes 5406720 | tf_op jit(solution)/shard_map/reduce_scatter | solution.py:117
  220.8 1.6 copy-start.2
  226.3 1.2 copy-start.3
  226.3 186.5 %reduce-scatter.3.cloned.1.call-start = ((), (), s32[]{:S(2)}) async-start(), calls=%async_computation.11 | async-start | bytes 5406720 | tf_op jit(solution)/shard_map/reduce_scatter | solution.py:111
  231.4 0.7 copy-start.4
  318.4 96.1 %all-to-all-start.5 = ((bf16[8,5,2048]{2,1,0:T(8,128)(2,1)}), bf16[8,5,2048]{2,1,0:T(8,128)(2,1)S(1)}, u32[]{:S(2)}, u32[]{:S(2)}) async-start(bf16[8,5,2048]{2,1,0:T(8,128)(2,1)} %reshape.100), calls=%async_computation.7 | async-start | bytes 524288 | tf_op jit(solution)/shard_map/all_to_all | solution.py:133
  414.5 17.5 %all-to-all-start.2 = ((bf16[8,5,2048]{2,1,0:T(8,128)(2,1)}), bf16[8,5,2048]{2,1,0:T(8,128)(2,1)S(1)}, u32[]{:S(2)}, u32[]{:S(2)}) async-start(bf16[8,5,2048]{2,1,0:T(8,128)(2,1)} %reshape.97), calls=%async_computation.3 | async-start | bytes 524288 | tf_op jit(solution)/shard_map/all_to_all | solution.py:126
  421.5 11.4 %copy-start.1 = (bf16[16,2048]{1,0:T(8,128)(2,1)S(1)}, bf16[16,2048]{1,0:T(8,128)(2,1)}, u32[]{:S(2)}) copy-start(bf16[16,2048]{1,0:T(8,128)(2,1)} %param.7) | copy-start | bytes 196612
Sparse Core Ops, SparseCore 0:
  30.7 48.4 all-gather.5
  82.4 52.1 all-gather.11
  136.4 38.4 all-gather.7
  176.5 37.1 all-gather.9
  226.4 90.2 reduce-scatter.4
  321.1 91.6 reduce-scatter.2
